TPU v7x, 32 devices: a whole 2x2x4 slice. The times are simulated.
32 devices in a mesh: group: 8 (over z, x), blk: 4 (over y, core).
Axes of the slice: x: 2, y: 2, z: 4, core: 2. Of those that a mesh axis runs over, the one named last changes fastest.
Arguments:
- sources: bfloat16 [32768, 512], P(('group', 'blk')), may hold values from -20 to 20
- targets: bfloat16 [256, 512], P(('group', 'blk')), may hold values from -20 to 20
- target_potential: bfloat16 [256], P(('group', 'blk')), may hold values from -1.5 to 1.5
- log_source_mass: float32 [32768], P(('group', 'blk')), may hold values from -3 to 0
- log_target_mass: float32 [256], P(('group', 'blk')), may hold values from -3 to 0
Outputs:
- source_potential: float32 [32768], P(('group', 'blk'))
- target_update: float32 [256], P(('group', 'blk'))
All inputs are finite; a program needn't handle non-finite values.
Results may differ from a plain program's by a relative error of at most 0.0003.
Values may be sent and summed in bfloat16 or wider, within the bound.
No kernel may reach another device: no remote copies, remote signals or barrier semaphores. Data moves between devices by JAX's collectives and lax.ppermute only.
A program may use at most 64 MiB of HBM per device.

v0:
```python
import jax
import jax.numpy as jnp
from jax import lax
from jax.sharding import PartitionSpec as P

epsilon = 0.05


def passed_along(block, axis, distance):
    devices = range(lax.axis_size(axis))
    route = [((i - distance) % len(devices), i) for i in devices]
    return lax.ppermute(block, axis, route)


def merged(x, axis, combine):
    everything = jax.tree.map(lambda part: lax.all_gather(part, axis), x)
    first = jax.tree.map(lambda part: part[0], everything)

    def hop(k, so_far):
        return combine(so_far, jax.tree.map(lambda part: part[k], everything))

    return lax.fori_loop(1, lax.axis_size(axis), hop, first)


def scores(source_rows, target_rows, target_pots):
    features = source_rows.shape[1]
    offset = target_pots.astype(jnp.float32) / epsilon - jnp.sum(
        jnp.square(target_rows.astype(jnp.float32)), 1
    ) / (features * epsilon)
    products = lax.dot_general(
        source_rows, target_rows, (((1,), (1,)), ((), ())), preferred_element_type=jnp.float32
    )
    return products * (2.0 / (features * epsilon)) + offset[None, :]


def split_blocks(target_rows, target_pots):
    row_count = target_rows.shape[0]
    block_width = 512 if row_count % 512 == 0 else row_count
    return (
        target_rows.reshape(row_count // block_width, block_width, target_rows.shape[1]),
        target_pots.reshape(row_count // block_width, block_width),
    )


def row_fold(running, source_rows, target_rows, target_pots):

    def advance(state, pieces):
        logits = scores(source_rows, pieces[0], pieces[1])
        run_max, run_sum = state
        new_max = jnp.maximum(run_max, jnp.max(logits, 1))
        new_sum = run_sum * jnp.exp(run_max - new_max) + jnp.sum(
            jnp.exp(logits - new_max[:, None]), 1
        )
        return ((new_max, new_sum), None)

    return lax.scan(advance, running, split_blocks(target_rows, target_pots))[0]


def column_parts(source_rows, source_dual, target_rows, target_pots):

    def single(pieces):
        logits = scores(source_rows, pieces[0], pieces[1])
        logits = logits - pieces[1].astype(jnp.float32)[None, :] / epsilon + source_dual[:, None]
        col_max = jnp.max(logits, 0)
        return (col_max, jnp.sum(jnp.exp(logits - col_max[None, :]), 0))

    col_max, col_sum = lax.map(single, split_blocks(target_rows, target_pots))
    return (col_max.reshape(-1), col_sum.reshape(-1))


def combine(first, second):
    new_max = jnp.maximum(first[0], second[0])
    return (
        new_max,
        first[1] * jnp.exp(first[0] - new_max) + second[1] * jnp.exp(second[0] - new_max),
    )


def per_device(sources, targets, target_potential, log_source_mass, log_target_mass):
    source_count = sources.shape[0]
    target_count = targets.shape[0]
    group_count = lax.axis_size("group")
    cycle_size = lax.axis_size("blk")
    initial = (
        jnp.full((source_count,), -1e30, jnp.float32),
        jnp.zeros((source_count,), jnp.float32),
    )
    gathered = (
        lax.all_gather(targets, "group", axis=0, tiled=True),
        lax.all_gather(target_potential, "group", axis=0, tiled=True),
    )
    own_block = lax.axis_index("blk")
    held = [(own_block, gathered)]
    forward_set = gathered
    backward_set = gathered
    for distance in range(1, cycle_size // 2 + 1):
        forward_set = passed_along((forward_set[0], forward_set[1]), "blk", 1)
        held.append(((own_block - distance) % cycle_size, forward_set))
        if distance <= (cycle_size - 1) // 2:
            backward_set = passed_along((backward_set[0], backward_set[1]), "blk", -1)
            held.append(((own_block + distance) % cycle_size, backward_set))
    running = initial
    for position, pieces in held:
        running = row_fold(running, sources, pieces[0], pieces[1])
    source_dual = log_source_mass - (running[0] + jnp.log(running[1]))
    grid_max = jnp.zeros((group_count, cycle_size, target_count), jnp.float32)
    grid_sum = jnp.zeros((group_count, cycle_size, target_count), jnp.float32)
    for position, pieces in held:
        part_max, part_sum = column_parts(sources, source_dual, pieces[0], pieces[1])
        where_put = (0, position, 0)
        grid_max = lax.dynamic_update_slice(
            grid_max, part_max.reshape(group_count, 1, target_count), where_put
        )
        grid_sum = lax.dynamic_update_slice(
            grid_sum, part_sum.reshape(group_count, 1, target_count), where_put
        )
    col_max = grid_max.reshape(-1)
    col_sum = grid_sum.reshape(-1)
    first_owned = (lax.axis_index("group") * cycle_size + lax.axis_index("blk")) * target_count
    total_max, total_sum = merged((col_max, col_sum), ("group", "blk"), combine)
    owned_max = lax.dynamic_slice_in_dim(total_max, first_owned, target_count)
    owned_sum = lax.dynamic_slice_in_dim(total_sum, first_owned, target_count)
    features = sources.shape[1]
    source_potential = (
        epsilon * source_dual + jnp.sum(jnp.square(sources.astype(jnp.float32)), 1) / features
    )
    target_update = epsilon * (log_target_mass - (owned_max + jnp.log(owned_sum)))
    return (source_potential, target_update)


def solution(mesh):
    return jax.shard_map(
        per_device,
        mesh=mesh,
        in_specs=(
            P(("group", "blk"), None),
            P(("group", "blk"), None),
            P(("group", "blk")),
            P(("group", "blk")),
            P(("group", "blk")),
        ),
        out_specs=(P(("group", "blk")), P(("group", "blk"))),
        check_vma=False,
    )
```

profile of v0, /device:TPU:0, one launch (start us, length us, event | category | flops | bytes accessed | tf_op | source)
XLA Modules:
  0.0 147.5 jit_solution(8099603570743714564)
XLA Ops:
  0.6 32.6 %all_gather.12 = bf16[64,512]{1,0:T(8,128)(2,1)S(1)} all-gather(bf16[8,512]{1,0:T(8,128)(2,1)} %param.8), channel_id=1, replica_groups=mesh['group'=8,'blk'=4] {'group'}, dimensions={0}, use_global_device_ids=true | all-gather | bytes 73728 | tf_op jit(solution)/shard_map/all_gather | solution.py:89
  33.3 1.7 %collective-permute-start.2 = (bf16[64,512]{1,0:T(8,128)(2,1)S(1)}, bf16[64,512]{1,0:T(8,128)(2,1)S(1)}, u32[]{:S(2)}, u32[]{:S(2)}) collective-permute-start(bf16[64,512]{1,0:T(8,128)(2,1)S(1)} %all_gather.12), channel_id=1, source_target_pairs={{1,0},{2,1},{3,2},{0,3},{5,4},{6,5},{7,6},{4,7},{9,8},{10,9},{11,1... | collective-permute-start | bytes 196616 | tf_op jit(solution)/shard_map/ppermute | solution.py:12
  35.0 1.2 dynamic-slice.8
  36.9 0.9 dynamic-update-slice
  37.8 21.3 %all-reduce = bf16[64]{0:T(256)(128)(2,1)S(1)} all-reduce(bf16[64]{0:T(256)(128)(2,1)S(1)} %dynamic-update-slice), channel_id=1, replica_groups=mesh['group'=8,'blk'=4] {'group'}, use_global_device_ids=true, to_apply=%add | all-reduce | flops 64 | bytes 256
  59.1 1.7 %collective-permute-start.3 = (bf16[64]{0:T(256)(128)(2,1)S(1)}, bf16[64]{0:T(256)(128)(2,1)S(1)}, u32[]{:S(2)}, u32[]{:S(2)}) collective-permute-start(bf16[64]{0:T(256)(128)(2,1)S(1)} %all-reduce), channel_id=1, source_target_pairs={{1,0},{2,1},{3,2},{0,3},{5,4},{6,5},{7,6},{4,7},{9,8},{10,9},{11,1... | collective-permute-start | bytes 392 | tf_op jit(solution)/shard_map/ppermute | solution.py:12
  60.9 0.1 multiply_reduce_fusion.4
  61.0 1.7 %fusion.14 = (f32[1024]{0:T(1024)S(1)}, f32[1024,64]{0,1:T(8,128)S(1)}) fusion(f32[64]{0:T(128)S(1)} %get-tuple-element.326, bf16[1024,512]{1,0:T(8,128)(2,1)} %param.7, bf16[64,512]{1,0:T(8,128)(2,1)S(1)} %all_gather.12), kind=kOutput, calls=%fused_computation.51 | convolution fusion | flops 67304448 | bytes 1380608 | tf_op jit(solution)/shard_map/while/body/eval_jaxpr/dot_general | solution.py:30
  62.7 0.3 multiply_reduce_fusion
  63.1 1.6 %collective-permute-start.4 = (bf16[64,512]{1,0:T(8,128)(2,1)S(1)}, bf16[64,512]{1,0:T(8,128)(2,1)S(1)}, u32[]{:S(2)}, u32[]{:S(2)}) collective-permute-start(bf16[64,512]{1,0:T(8,128)(2,1)S(1)} %collective-permute-done), channel_id=1, source_target_pairs={{3,0},{0,1},{1,2},{2,3},{7,4},{4,5},{5,6},{6,7},{11,8},{8,9},{9,10... | collective-permute-start | bytes 196616 | tf_op jit(solution)/shard_map/ppermute | solution.py:12
  64.7 0.1 multiply_reduce_fusion.3
  64.8 0.5 fusion.13
  65.3 0.1 multiply_reduce_fusion.2
  65.5 0.5 fusion.12
  65.9 0.9 collective-permute-done.4
  66.9 0.1 multiply_reduce_fusion.1
  67.0 0.5 fusion.11
  67.5 0.1 exponential_reduce_fusion.4
  67.6 0.1 exponential_reduce_fusion.6
  67.7 0.6 multiply_add_fusion.1
  68.3 0.2 fusion.7
  68.5 0.3 exponential_reduce_fusion
  68.9 0.3 exponential_reduce_fusion.1
  69.1 0.1 reshape_reshape.29
  69.2 0.1 reshape_reshape.28
  69.3 0.1 reshape_reshape.30
  69.7 0.1 reshape.118
  69.7 37.9 %all-gather.1 = f32[32,1,256]{2,1,0:T(1,128)S(1)} all-gather(f32[1,1,256]{2,1,0:T(1,128)S(1)} %reshape.118), channel_id=1, replica_groups=mesh['group'=8,'blk'=4] {'group','blk'}, dimensions={0}, use_global_device_ids=true | all-gather | bytes 33792 | tf_op jit(solution)/shard_map/all_gather | solution.py:16
  108.1 0.1 reshape.116
  108.2 36.8 %all-gather = f32[32,1,256]{2,1,0:T(1,128)S(1)} all-gather(f32[1,1,256]{2,1,0:T(1,128)S(1)} %reshape.116), channel_id=1, replica_groups=mesh['group'=8,'blk'=4] {'group','blk'}, dimensions={0}, use_global_device_ids=true | all-gather | bytes 33792 | tf_op jit(solution)/shard_map/all_gather | solution.py:16
  145.1 1.8 %while.11 = (s32[]{:T(128)}, f32[256]{0:T(256)S(1)}, f32[256]{0:T(256)S(1)}, f32[32,256]{1,0:T(8,128)S(1)}, f32[32,256]{1,0:T(8,128)S(1)}, /*index=5*/s32[]{:T(128)}, s32[]{:T(128)}, s32[]{:T(128)}) while((s32[]{:T(128)}, f32[256]{0:T(256)S(1)}, f32[256]{0:T(256)S(1)}, f32[32,256]{1,0:T(8,128)S(1)}, f32[32,256]{1,0:T(8,128)S(1)}, ...), condition=%wide.region_22.23_spmd, body=%wide.region_21.22_spmd.sunk | while | flops 1541 | bytes 10371 | solution.py:22
  146.9 0.6 subtract_multiply_fusion
  (101 shorter events, 1.9 us)
Async XLA Ops:
  0.6 62.0 %copy-start = (bf16[1024,512]{1,0:T(8,128)(2,1)S(1)}, bf16[1024,512]{1,0:T(8,128)(2,1)}, u32[]{:S(2)}) copy-start(bf16[1024,512]{1,0:T(8,128)(2,1)} %param.7) | copy-start | bytes 3145732
  33.3 29.8 %collective-permute-start = (bf16[64,512]{1,0:T(8,128)(2,1)S(1)}, bf16[64,512]{1,0:T(8,128)(2,1)S(1)}, u32[]{:S(2)}, u32[]{:S(2)}) collective-permute-start(bf16[64,512]{1,0:T(8,128)(2,1)S(1)} %all_gather.12), channel_id=1, source_target_pairs={{3,0},{0,1},{1,2},{2,3},{7,4},{4,5},{5,6},{6,7},{11,8},{8,9},{9,10... | collective-permute-start | bytes 196616 | tf_op jit(solution)/shard_map/ppermute | solution.py:12
  33.3 32.0 %collective-permute-start.2 = (bf16[64,512]{1,0:T(8,128)(2,1)S(1)}, bf16[64,512]{1,0:T(8,128)(2,1)S(1)}, u32[]{:S(2)}, u32[]{:S(2)}) collective-permute-start(bf16[64,512]{1,0:T(8,128)(2,1)S(1)} %all_gather.12), channel_id=1, source_target_pairs={{1,0},{2,1},{3,2},{0,3},{5,4},{6,5},{7,6},{4,7},{9,8},{10,9},{11,1... | collective-permute-start | bytes 196616 | tf_op jit(solution)/shard_map/ppermute | solution.py:12
  59.1 3.9 %collective-permute-start.1 = (bf16[64]{0:T(256)(128)(2,1)S(1)}, bf16[64]{0:T(256)(128)(2,1)S(1)}, u32[]{:S(2)}, u32[]{:S(2)}) collective-permute-start(bf16[64]{0:T(256)(128)(2,1)S(1)} %all-reduce), channel_id=1, source_target_pairs={{3,0},{0,1},{1,2},{2,3},{7,4},{4,5},{5,6},{6,7},{11,8},{8,9},{9,10... | collective-permute-start | bytes 392 | tf_op jit(solution)/shard_map/ppermute | solution.py:12
  59.1 6.3 %collective-permute-start.3 = (bf16[64]{0:T(256)(128)(2,1)S(1)}, bf16[64]{0:T(256)(128)(2,1)S(1)}, u32[]{:S(2)}, u32[]{:S(2)}) collective-permute-start(bf16[64]{0:T(256)(128)(2,1)S(1)} %all-reduce), channel_id=1, source_target_pairs={{1,0},{2,1},{3,2},{0,3},{5,4},{6,5},{7,6},{4,7},{9,8},{10,9},{11,1... | collective-permute-start | bytes 392 | tf_op jit(solution)/shard_map/ppermute | solution.py:12
  63.0 3.9 %collective-permute-start.5 = (bf16[64]{0:T(256)(128)(2,1)S(1)}, bf16[64]{0:T(256)(128)(2,1)S(1)}, u32[]{:S(2)}, u32[]{:S(2)}) collective-permute-start(bf16[64]{0:T(256)(128)(2,1)S(1)} %collective-permute-done.1), channel_id=1, source_target_pairs={{3,0},{0,1},{1,2},{2,3},{7,4},{4,5},{5,6},{6,7},{11,8},{8,9},{9,10... | collective-permute-start | bytes 392 | tf_op jit(solution)/shard_map/ppermute | solution.py:12
  63.1 3.7 %collective-permute-start.4 = (bf16[64,512]{1,0:T(8,128)(2,1)S(1)}, bf16[64,512]{1,0:T(8,128)(2,1)S(1)}, u32[]{:S(2)}, u32[]{:S(2)}) collective-permute-start(bf16[64,512]{1,0:T(8,128)(2,1)S(1)} %collective-permute-done), channel_id=1, source_target_pairs={{3,0},{0,1},{1,2},{2,3},{7,4},{4,5},{5,6},{6,7},{11,8},{8,9},{9,10... | collective-permute-start | bytes 196616 | tf_op jit(solution)/shard_map/ppermute | solution.py:12
  67.0 0.7 copy-start.1
  68.5 78.3 %copy-start.2 = (f32[8]{0:T(128)S(1)}, f32[8]{0:T(128)}, u32[]{:S(2)}) copy-start(f32[8]{0:T(128)} %param.11) | copy-start | bytes 100
where the time goes:
time: 148 us; the launch traced here: 147 us
  blocking collectives  129 us (87%)
  starting transfers between devices  5.19 us (4%)
  local copies, waits for them, and re-layouts  3.66 us (2%)
  other arithmetic  3.62 us (2%)
  matrix products  3.04 us (2%)
  between operations  1.56 us (1%)
    all_gather x2, blocking collectives, merged(): everything = jax.tree.map(lambda part: lax.all_gather(part, axis), x)  74.7 us
    all_gather x1, blocking collectives, per_device(): lax.all_gather(targets, 'group', axis=0, tiled=True)  32.6 us
    unnamed x1, blocking collectives  21.3 us
    ppermute x6, starting transfers between devices, passed_along(): return lax.ppermute(block, axis, route)  5.19 us
    dot_general x4, matrix products, scores(): lax.dot_general(source_rows, target_rows, (((1,), (1,)), ((), ())), prefe...  3.04 us
  transfers between devices with their start and end apart: 6, of which 1 were waited for; matrix products, arithmetic and copies ran while one was open for 4% of the time, Pallas kernels for 0%

commit v1 on v0

--- a/solution.py
+++ b/solution.py
@@ -4,6 +4,35 @@
 from jax.sharding import PartitionSpec as P
 
 epsilon = 0.05
+
+
+def frames_process(work_x):
+    bus_axis = "group"
+    all_values, new, p_next = (lax.axis_size(bus_axis), lax.axis_index(bus_axis), work_x.shape[0])
+    inbox = [nth * all_values if src_i == 0 else nth for src_i, nth in enumerate(work_x.shape)]
+    now = lax.dynamic_update_slice_in_dim(
+        jnp.zeros(inbox, work_x.dtype), work_x, new * p_next, axis=0
+    )
+    left_arr = small = work_x
+    for m in range(1, all_values // 2 + 1):
+        left_arr = lax.ppermute(
+            left_arr,
+            axis_name=bus_axis,
+            perm=[(src_i, (src_i + 1) % all_values) for src_i in range(all_values)],
+        )
+        now = lax.dynamic_update_slice_in_dim(
+            now, left_arr, (new - m) % all_values * p_next, axis=0
+        )
+        if 2 * m < all_values:
+            small = lax.ppermute(
+                small,
+                axis_name=bus_axis,
+                perm=[(src_i, (src_i - 1) % all_values) for src_i in range(all_values)],
+            )
+            now = lax.dynamic_update_slice_in_dim(
+                now, small, (new + m) % all_values * p_next, axis=0
+            )
+    return now
 
 
 def passed_along(block, axis, distance):
@@ -86,7 +115,7 @@
         jnp.zeros((source_count,), jnp.float32),
     )
     gathered = (
-        lax.all_gather(targets, "group", axis=0, tiled=True),
+        frames_process(targets),
         lax.all_gather(target_potential, "group", axis=0, tiled=True),
     )
     own_block = lax.axis_index("blk")

time: 148 us -> 140 us (0.946)
  blocking collectives: 129 us -> 93.8 us
  starting transfers between devices: 5.19 us -> 19.3 us
  waiting for transfers between devices: 0.95 us -> 13.7 us
    all_gather x1 -> x0, blocking collectives: 32.6 us -> none  [per_device(): lax.all_gather(targets, 'group', axis=0, tiled=True)]
    ppermute x0 -> x7, starting transfers between devices: none -> 15.6 us  [the longest x3 12.5 us: frames_process(): lax.ppermute(small, axis_name=bus_axis, perm=[(src_i, (src_i - 1) % all_v...]
    ppermute x0 -> x7, waiting for transfers between devices: none -> 9.56 us  [the longest x4 9.56 us: frames_process(): lax.ppermute(left_arr, axis_name=bus_axis, perm=[(src_i, (src_i + 1) % al...]
    ppermute x6, waiting for transfers between devices: 0.95 us -> 4.09 us  [passed_along(): return lax.ppermute(block, axis, route)]
    unnamed x1, blocking collectives: 21.3 us -> 19.1 us
    ppermute x6, starting transfers between devices: 5.19 us -> 3.68 us  [passed_along(): return lax.ppermute(block, axis, route)]
  transfers between devices with their start and end apart: 6 -> 13, of which waited for: 1 -> 5; matrix products, arithmetic and copies ran while one was open for 4% -> 4% of each run, Pallas kernels for 0% -> 0%
where the time goes in v1:
time: 140 us
  blocking collectives  93.8 us (67%)
  starting transfers between devices  19.3 us (14%)
  waiting for transfers between devices  13.7 us (10%)
  other arithmetic  4.84 us (3%)
  local copies, waits for them, and re-layouts  3.7 us (3%)
  matrix products  1.8 us (1%)
  between operations  1.74 us (1%)
    all_gather x2, blocking collectives, merged(): everything = jax.tree.map(lambda part: lax.all_gather(part, axis), x)  74.7 us
    unnamed x1, blocking collectives  19.1 us
    ppermute x3, starting transfers between devices, frames_process(): lax.ppermute(small, axis_name=bus_axis, perm=[(src_i, (src_i - 1) % all_v...  12.5 us
    ppermute x4, waiting for transfers between devices, frames_process(): lax.ppermute(left_arr, axis_name=bus_axis, perm=[(src_i, (src_i + 1) % al...  9.56 us
    ppermute x6, waiting for transfers between devices, passed_along(): return lax.ppermute(block, axis, route)  4.09 us
    ppermute x6, starting transfers between devices, passed_along(): return lax.ppermute(block, axis, route)  3.68 us
    ppermute x4, starting transfers between devices, frames_process(): lax.ppermute(left_arr, axis_name=bus_axis, perm=[(src_i, (src_i + 1) % al...  3.11 us
  transfers between devices with their start and end apart: 13, of which 5 were waited for; matrix products, arithmetic and copies ran while one was open for 4% of the time, Pallas kernels for 0%

profile of v1, /device:TPU:0, one launch (start us, length us, event | category | flops | bytes accessed | tf_op | source)
XLA Modules:
  0.0 139.6 jit_solution(5346258006883296176)
XLA Ops:
  0.7 3.0 %collective-permute-start = (bf16[8,512]{1,0:T(8,128)(2,1)}, bf16[8,512]{1,0:T(8,128)(2,1)S(1)}, u32[]{:S(2)}, u32[]{:S(2)}) collective-permute-start(bf16[8,512]{1,0:T(8,128)(2,1)} %param.8), channel_id=1, source_target_pairs={{0,4},{4,8},{8,12},{12,16},{16,20},{20,24},{24,28},{28,0},{1,5},{5... | collective-permute-start | bytes 24584 | tf_op jit(solution)/shard_map/ppermute | solution.py:18
  3.6 3.1 %collective-permute-start.1 = (bf16[8,512]{1,0:T(8,128)(2,1)}, bf16[8,512]{1,0:T(8,128)(2,1)S(1)}, u32[]{:S(2)}, u32[]{:S(2)}) collective-permute-start(bf16[8,512]{1,0:T(8,128)(2,1)} %param.8), channel_id=1, source_target_pairs={{0,28},{4,0},{8,4},{12,8},{16,12},{20,16},{24,20},{28,24},{1,29},{... | collective-permute-start | bytes 24584 | tf_op jit(solution)/shard_map/ppermute | solution.py:27
  6.7 1.2 dynamic-slice.8
  8.6 0.9 dynamic-update-slice
  9.5 19.1 %all-reduce = bf16[64]{0:T(256)(128)(2,1)S(1)} all-reduce(bf16[64]{0:T(256)(128)(2,1)S(1)} %dynamic-update-slice), channel_id=1, replica_groups=mesh['group'=8,'blk'=4] {'group'}, use_global_device_ids=true, to_apply=%add | all-reduce | flops 64 | bytes 256
  28.6 1.7 %collective-permute-start.10 = (bf16[64]{0:T(256)(128)(2,1)S(1)}, bf16[64]{0:T(256)(128)(2,1)S(1)}, u32[]{:S(2)}, u32[]{:S(2)}) collective-permute-start(bf16[64]{0:T(256)(128)(2,1)S(1)} %all-reduce), channel_id=1, source_target_pairs={{1,0},{2,1},{3,2},{0,3},{5,4},{6,5},{7,6},{4,7},{9,8},{10,9},{11,1... | collective-permute-start | bytes 392 | tf_op jit(solution)/shard_map/ppermute | solution.py:41
  30.4 1.5 %multiply_reduce_fusion = f32[1024]{0:T(1024)S(1)} fusion(bf16[1024,512]{1,0:T(8,128)(2,1)} %param.7), kind=kLoop, calls=%fused_computation.3 | loop fusion | flops 1571840 | bytes 1052672 | tf_op jit(solution)/shard_map/reduce_sum | solution.py:154
  32.2 0.1 collective-permute-start.2
  32.3 4.7 %collective-permute-start.3 = (bf16[8,512]{1,0:T(8,128)(2,1)S(1)}, bf16[8,512]{1,0:T(8,128)(2,1)S(1)}, u32[]{:S(2)}, u32[]{:S(2)}) collective-permute-start(bf16[8,512]{1,0:T(8,128)(2,1)S(1)} %collective-permute-done.1), channel_id=1, source_target_pairs={{0,28},{4,0},{8,4},{12,8},{16,12},{20,16},{24,20},{28,24},{1,29},{... | collective-permute-start | bytes 24584 | tf_op jit(solution)/shard_map/ppermute | solution.py:27
  37.0 1.6 %collective-permute-done.2 = bf16[8,512]{1,0:T(8,128)(2,1)S(1)} collective-permute-done((bf16[8,512]{1,0:T(8,128)(2,1)S(1)}, bf16[8,512]{1,0:T(8,128)(2,1)S(1)}, u32[]{:S(2)}, u32[]{:S(2)}) %collective-permute-start.2) | collective-permute-done | bytes 8224 | tf_op jit(solution)/shard_map/ppermute | solution.py:18
  38.6 4.7 %collective-permute-start.5 = (bf16[8,512]{1,0:T(8,128)(2,1)S(1)}, bf16[8,512]{1,0:T(8,128)(2,1)S(1)}, u32[]{:S(2)}, u32[]{:S(2)}) collective-permute-start(bf16[8,512]{1,0:T(8,128)(2,1)S(1)} %collective-permute-done.3), channel_id=1, source_target_pairs={{0,28},{4,0},{8,4},{12,8},{16,12},{20,16},{24,20},{28,24},{1,29},{... | collective-permute-start | bytes 24584 | tf_op jit(solution)/shard_map/ppermute | solution.py:27
  43.3 1.6 %collective-permute-done.4 = bf16[8,512]{1,0:T(8,128)(2,1)S(1)} collective-permute-done((bf16[8,512]{1,0:T(8,128)(2,1)S(1)}, bf16[8,512]{1,0:T(8,128)(2,1)S(1)}, u32[]{:S(2)}, u32[]{:S(2)}) %collective-permute-start.4) | collective-permute-done | bytes 8224 | tf_op jit(solution)/shard_map/ppermute | solution.py:18
  44.9 6.3 %collective-permute-done.6 = bf16[8,512]{1,0:T(8,128)(2,1)S(1)} collective-permute-done((bf16[8,512]{1,0:T(8,128)(2,1)S(1)}, bf16[8,512]{1,0:T(8,128)(2,1)S(1)}, u32[]{:S(2)}, u32[]{:S(2)}) %collective-permute-start.6) | collective-permute-done | bytes 8224 | tf_op jit(solution)/shard_map/ppermute | solution.py:18
  51.3 0.1 multiply_reduce_fusion.4
  51.4 1.7 %collective-permute-start.9 = (bf16[64,512]{1,0:T(8,128)(2,1)S(1)}, bf16[64,512]{1,0:T(8,128)(2,1)S(1)}, u32[]{:S(2)}, u32[]{:S(2)}) collective-permute-start(bf16[64,512]{1,0:T(8,128)(2,1)S(1)} %constant_dynamic-update-slice_fusion), channel_id=1, source_target_pairs={{1,0},{2,1},{3,2},{0,3},{5,4},{6,5},{7,6},{4,7},{9,8},{10,9},{11,1... | collective-permute-start | bytes 196616 | tf_op jit(solution)/shard_map/ppermute | solution.py:41
  53.2 0.4 fusion.14
  53.6 1.5 %collective-permute-done.7 = bf16[64,512]{1,0:T(8,128)(2,1)S(1)} collective-permute-done((bf16[64,512]{1,0:T(8,128)(2,1)S(1)}, bf16[64,512]{1,0:T(8,128)(2,1)S(1)}, u32[]{:S(2)}, u32[]{:S(2)}) %collective-permute-start.7) | collective-permute-done | bytes 65568 | tf_op jit(solution)/shard_map/ppermute | solution.py:41
  55.1 0.1 multiply_reduce_fusion.3
  55.3 0.5 fusion.13
  55.8 0.1 multiply_reduce_fusion.2
  55.9 0.5 fusion.12
  56.4 2.6 %collective-permute-done.11 = bf16[64,512]{1,0:T(8,128)(2,1)S(1)} collective-permute-done((bf16[64,512]{1,0:T(8,128)(2,1)S(1)}, bf16[64,512]{1,0:T(8,128)(2,1)S(1)}, u32[]{:S(2)}, u32[]{:S(2)}) %collective-permute-start.11) | collective-permute-done | bytes 65568 | tf_op jit(solution)/shard_map/ppermute | solution.py:41
  59.0 0.1 multiply_reduce_fusion.1
  59.1 0.5 fusion.11
  59.8 0.6 multiply_add_fusion.1
  60.4 0.2 fusion.7
  60.7 0.3 exponential_reduce_fusion
  61.0 0.3 exponential_reduce_fusion.1
  61.9 37.9 %all-gather.1 = f32[32,1,256]{2,1,0:T(1,128)S(1)} all-gather(f32[1,1,256]{2,1,0:T(1,128)S(1)} %reshape.118), channel_id=1, replica_groups=mesh['group'=8,'blk'=4] {'group','blk'}, dimensions={0}, use_global_device_ids=true | all-gather | bytes 33792 | tf_op jit(solution)/shard_map/all_gather | solution.py:45
  100.3 36.8 %all-gather = f32[32,1,256]{2,1,0:T(1,128)S(1)} all-gather(f32[1,1,256]{2,1,0:T(1,128)S(1)} %reshape.116), channel_id=1, replica_groups=mesh['group'=8,'blk'=4] {'group','blk'}, dimensions={0}, use_global_device_ids=true | all-gather | bytes 33792 | tf_op jit(solution)/shard_map/all_gather | solution.py:45
  137.2 1.8 %while.11 = (s32[]{:T(128)}, f32[256]{0:T(256)S(1)}, f32[256]{0:T(256)S(1)}, f32[32,256]{1,0:T(8,128)S(1)}, f32[32,256]{1,0:T(8,128)S(1)}, /*index=5*/s32[]{:T(128)}, s32[]{:T(128)}, s32[]{:T(128)}) while((s32[]{:T(128)}, f32[256]{0:T(256)S(1)}, f32[256]{0:T(256)S(1)}, f32[32,256]{1,0:T(8,128)S(1)}, f32[32,256]{1,0:T(8,128)S(1)}, ...), condition=%wide.region_22.23_spmd, body=%wide.region_21.22_spmd.sunk | while | flops 1541 | bytes 10371 | solution.py:51
  139.0 0.6 subtract_multiply_fusion
  (125 shorter events, 2.7 us)
Async XLA Ops:
  0.6 31.3 %copy-start.1 = (bf16[8,512]{1,0:T(8,128)(2,1)S(1)}, bf16[8,512]{1,0:T(8,128)(2,1)}, u32[]{:S(2)}) copy-start(bf16[8,512]{1,0:T(8,128)(2,1)} %param.8) | copy-start | bytes 24580
  0.6 52.6 %copy-start = (bf16[1024,512]{1,0:T(8,128)(2,1)S(1)}, bf16[1024,512]{1,0:T(8,128)(2,1)}, u32[]{:S(2)}) copy-start(bf16[1024,512]{1,0:T(8,128)(2,1)} %param.7) | copy-start | bytes 3145732
  0.7 31.5 %collective-permute-start = (bf16[8,512]{1,0:T(8,128)(2,1)}, bf16[8,512]{1,0:T(8,128)(2,1)S(1)}, u32[]{:S(2)}, u32[]{:S(2)}) collective-permute-start(bf16[8,512]{1,0:T(8,128)(2,1)} %param.8), channel_id=1, source_target_pairs={{0,4},{4,8},{8,12},{12,16},{16,20},{20,24},{24,28},{28,0},{1,5},{5... | collective-permute-start | bytes 24584 | tf_op jit(solution)/shard_map/ppermute | solution.py:18
  3.6 28.6 %collective-permute-start.1 = (bf16[8,512]{1,0:T(8,128)(2,1)}, bf16[8,512]{1,0:T(8,128)(2,1)S(1)}, u32[]{:S(2)}, u32[]{:S(2)}) collective-permute-start(bf16[8,512]{1,0:T(8,128)(2,1)} %param.8), channel_id=1, source_target_pairs={{0,28},{4,0},{8,4},{12,8},{16,12},{20,16},{24,20},{28,24},{1,29},{... | collective-permute-start | bytes 24584 | tf_op jit(solution)/shard_map/ppermute | solution.py:27
  28.6 3.5 %collective-permute-start.8 = (bf16[64]{0:T(256)(128)(2,1)S(1)}, bf16[64]{0:T(256)(128)(2,1)S(1)}, u32[]{:S(2)}, u32[]{:S(2)}) collective-permute-start(bf16[64]{0:T(256)(128)(2,1)S(1)} %all-reduce), channel_id=1, source_target_pairs={{3,0},{0,1},{1,2},{2,3},{7,4},{4,5},{5,6},{6,7},{11,8},{8,9},{9,10... | collective-permute-start | bytes 392 | tf_op jit(solution)/shard_map/ppermute | solution.py:41
  28.6 27.3 %collective-permute-start.10 = (bf16[64]{0:T(256)(128)(2,1)S(1)}, bf16[64]{0:T(256)(128)(2,1)S(1)}, u32[]{:S(2)}, u32[]{:S(2)}) collective-permute-start(bf16[64]{0:T(256)(128)(2,1)S(1)} %all-reduce), channel_id=1, source_target_pairs={{1,0},{2,1},{3,2},{0,3},{5,4},{6,5},{7,6},{4,7},{9,8},{10,9},{11,1... | collective-permute-start | bytes 392 | tf_op jit(solution)/shard_map/ppermute | solution.py:41
  32.1 27.0 %collective-permute-start.12 = (bf16[64]{0:T(256)(128)(2,1)S(1)}, bf16[64]{0:T(256)(128)(2,1)S(1)}, u32[]{:S(2)}, u32[]{:S(2)}) collective-permute-start(bf16[64]{0:T(256)(128)(2,1)S(1)} %collective-permute-done.8), channel_id=1, source_target_pairs={{3,0},{0,1},{1,2},{2,3},{7,4},{4,5},{5,6},{6,7},{11,8},{8,9},{9,10... | collective-permute-start | bytes 392 | tf_op jit(solution)/shard_map/ppermute | solution.py:41
  32.2 6.4 %collective-permute-start.2 = (bf16[8,512]{1,0:T(8,128)(2,1)S(1)}, bf16[8,512]{1,0:T(8,128)(2,1)S(1)}, u32[]{:S(2)}, u32[]{:S(2)}) collective-permute-start(bf16[8,512]{1,0:T(8,128)(2,1)S(1)} %collective-permute-done), channel_id=1, source_target_pairs={{0,4},{4,8},{8,12},{12,16},{16,20},{20,24},{24,28},{28,0},{1,5},{5... | collective-permute-start | bytes 24584 | tf_op jit(solution)/shard_map/ppermute | solution.py:18
  32.3 6.3 %collective-permute-start.3 = (bf16[8,512]{1,0:T(8,128)(2,1)S(1)}, bf16[8,512]{1,0:T(8,128)(2,1)S(1)}, u32[]{:S(2)}, u32[]{:S(2)}) collective-permute-start(bf16[8,512]{1,0:T(8,128)(2,1)S(1)} %collective-permute-done.1), channel_id=1, source_target_pairs={{0,28},{4,0},{8,4},{12,8},{16,12},{20,16},{24,20},{28,24},{1,29},{... | collective-permute-start | bytes 24584 | tf_op jit(solution)/shard_map/ppermute | solution.py:27
  38.6 6.3 %collective-permute-start.4 = (bf16[8,512]{1,0:T(8,128)(2,1)S(1)}, bf16[8,512]{1,0:T(8,128)(2,1)S(1)}, u32[]{:S(2)}, u32[]{:S(2)}) collective-permute-start(bf16[8,512]{1,0:T(8,128)(2,1)S(1)} %collective-permute-done.2), channel_id=1, source_target_pairs={{0,4},{4,8},{8,12},{12,16},{16,20},{20,24},{24,28},{28,0},{1,5},{5... | collective-permute-start | bytes 24584 | tf_op jit(solution)/shard_map/ppermute | solution.py:18
  38.6 6.3 %collective-permute-start.5 = (bf16[8,512]{1,0:T(8,128)(2,1)S(1)}, bf16[8,512]{1,0:T(8,128)(2,1)S(1)}, u32[]{:S(2)}, u32[]{:S(2)}) collective-permute-start(bf16[8,512]{1,0:T(8,128)(2,1)S(1)} %collective-permute-done.3), channel_id=1, source_target_pairs={{0,28},{4,0},{8,4},{12,8},{16,12},{20,16},{24,20},{28,24},{1,29},{... | collective-permute-start | bytes 24584 | tf_op jit(solution)/shard_map/ppermute | solution.py:27
  44.9 6.3 %collective-permute-start.6 = (bf16[8,512]{1,0:T(8,128)(2,1)S(1)}, bf16[8,512]{1,0:T(8,128)(2,1)S(1)}, u32[]{:S(2)}, u32[]{:S(2)}) collective-permute-start(bf16[8,512]{1,0:T(8,128)(2,1)S(1)} %collective-permute-done.4), channel_id=1, source_target_pairs={{0,4},{4,8},{8,12},{12,16},{16,20},{20,24},{24,28},{28,0},{1,5},{5... | collective-permute-start | bytes 24584 | tf_op jit(solution)/shard_map/ppermute | solution.py:18
  51.4 3.7 %collective-permute-start.7 = (bf16[64,512]{1,0:T(8,128)(2,1)S(1)}, bf16[64,512]{1,0:T(8,128)(2,1)S(1)}, u32[]{:S(2)}, u32[]{:S(2)}) collective-permute-start(bf16[64,512]{1,0:T(8,128)(2,1)S(1)} %constant_dynamic-update-slice_fusion), channel_id=1, source_target_pairs={{3,0},{0,1},{1,2},{2,3},{7,4},{4,5},{5,6},{6,7},{11,8},{8,9},{9,10... | collective-permute-start | bytes 196616 | tf_op jit(solution)/shard_map/ppermute | solution.py:41
  51.4 4.3 %collective-permute-start.9 = (bf16[64,512]{1,0:T(8,128)(2,1)S(1)}, bf16[64,512]{1,0:T(8,128)(2,1)S(1)}, u32[]{:S(2)}, u32[]{:S(2)}) collective-permute-start(bf16[64,512]{1,0:T(8,128)(2,1)S(1)} %constant_dynamic-update-slice_fusion), channel_id=1, source_target_pairs={{1,0},{2,1},{3,2},{0,3},{5,4},{6,5},{7,6},{4,7},{9,8},{10,9},{11,1... | collective-permute-start | bytes 196616 | tf_op jit(solution)/shard_map/ppermute | solution.py:41
  55.2 3.7 %collective-permute-start.11 = (bf16[64,512]{1,0:T(8,128)(2,1)S(1)}, bf16[64,512]{1,0:T(8,128)(2,1)S(1)}, u32[]{:S(2)}, u32[]{:S(2)}) collective-permute-start(bf16[64,512]{1,0:T(8,128)(2,1)S(1)} %collective-permute-done.7), channel_id=1, source_target_pairs={{3,0},{0,1},{1,2},{2,3},{7,4},{4,5},{5,6},{6,7},{11,8},{8,9},{9,10... | collective-permute-start | bytes 196616 | tf_op jit(solution)/shard_map/ppermute | solution.py:41
  59.1 0.7 copy-start.2
  60.6 78.3 %copy-start.3 = (f32[8]{0:T(128)S(1)}, f32[8]{0:T(128)}, u32[]{:S(2)}) copy-start(f32[8]{0:T(128)} %param.11) | copy-start | bytes 100
